TPU v7x, 256 devices: a whole 4x4x8 slice. The times are simulated.
256 devices in a mesh: gx: 32 (over x, y, core), gy: 8 (over z).
Axes of the slice: x: 4, y: 4, z: 8, core: 2. Of those that a mesh axis runs over, the one named last changes fastest.
Arguments:
- leaf_load: bfloat16 [65536, 384], P(('gx', 'gy')), may hold values from -6 to 6
- front_zero: bfloat16 [65536, 8192], P(('gx', 'gy')), may hold values from -0.046875 to 0.046875
- front_one: bfloat16 [32768, 8192], P(('gx', 'gy')), may hold values from -0.046875 to 0.046875
- front_two: bfloat16 [16384, 8192], P(('gx', 'gy')), may hold values from -0.046875 to 0.046875
- front_root: bfloat16 [8192, 8192], P(('gx', 'gy')), may hold values from -0.046875 to 0.046875
- load_one: float32 [32768, 384], P(('gx', 'gy')), may hold values from -6 to 6
- load_two: float32 [16384, 384], P(('gx', 'gy')), may hold values from -6 to 6
- load_root: float32 [8192, 384], P(('gx', 'gy')), may hold values from -6 to 6
- map_one: int32 [8192, 2], replicated, may hold values from 0 to 255
- map_two: int32 [8192, 2], replicated, may hold values from 0 to 127
- map_root: int32 [8192, 2], replicated, may hold values from 0 to 63
- adjoint: float32 [64, 128, 384], P('gx', 'gy'), may hold values from -6 to 6
Outputs:
- root_solution: float32 [8192, 384], P(('gx', 'gy'))
- gradient: float32 [64, 128, 384], P('gx', 'gy')
All inputs are finite; a program needn't handle non-finite values.
Results may differ from a plain program's by a relative error of at most 0.0055.
Values may be sent and summed in bfloat16 or wider, within the bound.
No kernel may reach another device: no remote copies, remote signals or barrier semaphores. Data moves between devices by JAX's collectives and lax.ppermute only.
A program may use at most 64 MiB of HBM per device.

v0:
```python
import jax
import jax.numpy as jnp
from jax import lax
from jax.sharding import PartitionSpec as P


def swapped(x, axis, distance):
    return lax.ppermute(x, axis, [(i, i ^ 1 << distance) for i in range(lax.axis_size(axis))])


def padded_2(cells, sides, width):
    for axis, dim in sides:
        count = lax.axis_size(axis)
        ends = count - 1
        head = lax.slice_in_dim(cells, 0, width, axis=dim)
        tail = lax.slice_in_dim(cells, cells.shape[dim] - width, cells.shape[dim], axis=dim)
        cells = jnp.concatenate(
            [
                lax.ppermute(tail, axis, [(i, (i + 1) % count) for i in range(ends)]),
                cells,
                lax.ppermute(head, axis, [((i + 1) % count, i) for i in range(ends)]),
            ],
            axis=dim,
        )
    return cells


def group_rows(values, bits):
    values = lax.all_gather(values, "gy", axis=0, tiled=True)
    column = lax.axis_index("gx")
    for bit in range(bits):
        other = swapped(values, "gx", bit)
        upper = column >> bit & 1 == 1
        values = jnp.where(
            upper, jnp.concatenate([other, values], 0), jnp.concatenate([values, other], 0)
        )
    return values


def local(
    leaf_load,
    front_zero,
    front_one,
    front_two,
    front_root,
    load_one,
    load_two,
    load_root,
    map_one,
    map_two,
    map_root,
    adjoint,
):
    leaf_bits = lax.axis_size("gx").bit_length() - 4
    fronts = (front_zero, front_one, front_two)
    loads = (load_one, load_two, load_root)
    mappings = (map_one, map_two, map_root)
    column = lax.axis_index("gx")
    row_index = lax.axis_index("gy")
    state = leaf_load
    for level in range(3):
        bits = leaf_bits + level
        whole = group_rows(state, bits)
        product = jnp.dot(fronts[level], whole, preferred_element_type=jnp.float32)
        other = swapped(product, "gx", bits)
        upper = column >> bits & 1 == 1
        first = jnp.where(upper, other, product)
        second = jnp.where(upper, product, other)
        half = product.shape[0] // 2
        position = column % 2 ** (bits + 1) * lax.axis_size("gy") + row_index
        local_map = lax.dynamic_slice_in_dim(mappings[level], position * half, half, 0)
        total = (
            loads[level]
            + jnp.take(first, local_map[:, 0], axis=0)
            + jnp.take(second, local_map[:, 1], axis=0)
        )
        state = total.astype(jnp.bfloat16)
    whole = group_rows(state, leaf_bits + 3)
    root_solution = jnp.dot(front_root, whole, preferred_element_type=jnp.float32)
    cells_x = adjoint.shape[0]
    cells_y = adjoint.shape[1]
    width = adjoint.shape[2]
    plane = root_solution.reshape(cells_x, cells_y, width)
    stacked = jnp.stack([plane, adjoint])
    padded = padded_2(stacked, (("gx", 1), ("gy", 2)), 1)
    padded_u = padded[0]
    padded_a = padded[1]
    gradient = jnp.zeros((cells_x, cells_y, width), jnp.float32)
    for lo_x, lo_y in ((2, 1), (0, 1), (1, 2), (1, 0)):
        near_u = padded_u[lo_x : lo_x + cells_x, lo_y : lo_y + cells_y]
        near_a = padded_a[lo_x : lo_x + cells_x, lo_y : lo_y + cells_y]
        gradient = gradient + (plane - near_u) * (adjoint - near_a)
    return (root_solution, gradient)


def solution(mesh):
    in_specs = (
        P(("gx", "gy"), None),
        P(("gx", "gy"), None),
        P(("gx", "gy"), None),
        P(("gx", "gy"), None),
        P(("gx", "gy"), None),
        P(("gx", "gy"), None),
        P(("gx", "gy"), None),
        P(("gx", "gy"), None),
        P(),
        P(),
        P(),
        P("gx", "gy", None),
    )
    out_specs = (P(("gx", "gy"), None), P("gx", "gy", None))
    return jax.shard_map(local, mesh=mesh, in_specs=in_specs, out_specs=out_specs, check_vma=False)
```

profile of v0, /device:TPU:34, one launch (start us, length us, event | category | flops | bytes accessed | tf_op | source)
XLA Modules:
  0.0 686.3 jit_solution(2727871176709467057)
XLA Ops:
  7.9 44.2 %all-gather.2.cloned.1.call-done = bf16[2048,384]{1,0:T(8,128)(2,1)} async-done(((bf16[256,384]{1,0:T(8,128)(2,1)}), bf16[2048,384]{1,0:T(8,128)(2,1)}) %all-gather.2.cloned.1.call-update) | async-done | bytes 1572880 | tf_op jit(solution)/shard_map/all_gather | solution.py:29
  55.8 5.5 maximum_select_fusion.8
  62.8 69.0 %collective-permute-done.1 = bf16[4096,384]{1,0:T(8,128)(2,1)} collective-permute-done((bf16[4096,384]{1,0:T(8,128)(2,1)}, bf16[4096,384]{1,0:T(8,128)(2,1)}, u32[]{:S(2)}, u32[]{:S(2)}) %collective-permute-start.1) | collective-permute-done | bytes 3145760 | tf_op jit(solution)/shard_map/ppermute | solution.py:8
  131.8 9.1 %fusion.28 = f32[256,384]{0,1:T(8,128)S(1)} fusion(bf16[256,8192]{1,0:T(8,128)(2,1)} %param.19, bf16[4096,384]{1,0:T(8,128)(2,1)} %maximum_select_fusion.8, bf16[4096,384]{1,0:T(8,128)(2,1)} %collective-permute-done.1, pred[]{:T(512)S(6)} %eq.17), kind=kOutput, calls=%fused_computation.45 | convolution fusion | flops 1638924288 | bytes 10878977 | tf_op jit(solution)/shard_map/dot_general | solution.py:64
  144.7 8.1 %collective-permute-done.2 = f32[256,384]{0,1:T(8,128)S(1)} collective-permute-done((f32[256,384]{0,1:T(8,128)S(1)}, f32[256,384]{0,1:T(8,128)S(1)}, u32[]{:S(2)}, u32[]{:S(2)}) %collective-permute-start.2) | collective-permute-done | bytes 393248 | tf_op jit(solution)/shard_map/ppermute | solution.py:8
  154.8 25.7 %all_gather.13 = bf16[1024,384]{1,0:T(8,128)(2,1)S(1)} all-gather(bf16[128,384]{1,0:T(8,128)(2,1)S(1)} %fusion.31), channel_id=1, replica_groups=mesh['gx'=32,'gy'=8] {'gy'}, dimensions={0}, use_global_device_ids=true | all-gather | bytes 884736 | tf_op jit(solution)/shard_map/all_gather | solution.py:29
  184.8 35.0 %collective-permute-done.4 = bf16[2048,384]{1,0:T(8,128)(2,1)S(1)} collective-permute-done((bf16[2048,384]{1,0:T(8,128)(2,1)S(1)}, bf16[2048,384]{1,0:T(8,128)(2,1)S(1)}, u32[]{:S(2)}, u32[]{:S(2)}) %collective-permute-start.4) | collective-permute-done | bytes 1572896 | tf_op jit(solution)/shard_map/ppermute | solution.py:8
  219.8 8.3 %maximum_select_fusion.9 = bf16[4096,384]{1,0:T(8,128)(2,1)} fusion(bf16[2048,384]{1,0:T(8,128)(2,1)S(1)} %maximum_select_fusion.12, bf16[2048,384]{1,0:T(8,128)(2,1)S(1)} %collective-permute-done.4, pred[]{:T(512)S(6)} %eq.17), kind=kLoop, calls=%fused_computation.39 | loop fusion | flops 14155776 | bytes 6291457 | tf_op jit(solution)/shard_map/jit(_where)/select_n | solution.py:34
  231.8 67.4 %collective-permute-done.5 = bf16[4096,384]{1,0:T(8,128)(2,1)} collective-permute-done((bf16[4096,384]{1,0:T(8,128)(2,1)}, bf16[4096,384]{1,0:T(8,128)(2,1)}, u32[]{:S(2)}, u32[]{:S(2)}) %collective-permute-start.5) | collective-permute-done | bytes 3145760 | tf_op jit(solution)/shard_map/ppermute | solution.py:8
  299.2 6.3 fusion.29
  306.4 5.1 collective-permute-done.6
  313.2 25.2 %all_gather.14 = bf16[512,384]{1,0:T(8,128)(2,1)S(1)} all-gather(bf16[64,384]{1,0:T(8,128)(2,1)S(1)} %fusion.32), channel_id=1, replica_groups=mesh['gx'=32,'gy'=8] {'gy'}, dimensions={0}, use_global_device_ids=true | all-gather | bytes 442368 | tf_op jit(solution)/shard_map/all_gather | solution.py:29
  342.0 18.1 %collective-permute-done.8 = bf16[1024,384]{1,0:T(8,128)(2,1)S(1)} collective-permute-done((bf16[1024,384]{1,0:T(8,128)(2,1)S(1)}, bf16[1024,384]{1,0:T(8,128)(2,1)S(1)}, u32[]{:S(2)}, u32[]{:S(2)}) %collective-permute-start.8) | collective-permute-done | bytes 786464 | tf_op jit(solution)/shard_map/ppermute | solution.py:8
  363.6 34.1 %collective-permute-done.9 = bf16[2048,384]{1,0:T(8,128)(2,1)S(1)} collective-permute-done((bf16[2048,384]{1,0:T(8,128)(2,1)S(1)}, bf16[2048,384]{1,0:T(8,128)(2,1)S(1)}, u32[]{:S(2)}, u32[]{:S(2)}) %collective-permute-start.9) | collective-permute-done | bytes 1572896 | tf_op jit(solution)/shard_map/ppermute | solution.py:8
  397.7 8.3 %maximum_select_fusion.10 = bf16[4096,384]{1,0:T(8,128)(2,1)} fusion(bf16[2048,384]{1,0:T(8,128)(2,1)S(1)} %maximum_select_fusion.13, bf16[2048,384]{1,0:T(8,128)(2,1)S(1)} %collective-permute-done.9, pred[]{:T(512)S(6)} %eq.16), kind=kLoop, calls=%fused_computation.40 | loop fusion | flops 14155776 | bytes 6291457 | tf_op jit(solution)/shard_map/jit(_where)/select_n | solution.py:34
  407.3 67.4 %collective-permute-done.10 = bf16[4096,384]{1,0:T(8,128)(2,1)} collective-permute-done((bf16[4096,384]{1,0:T(8,128)(2,1)}, bf16[4096,384]{1,0:T(8,128)(2,1)}, u32[]{:S(2)}, u32[]{:S(2)}) %collective-permute-start.10) | collective-permute-done | bytes 3145760 | tf_op jit(solution)/shard_map/ppermute | solution.py:8
  474.7 6.2 fusion.30
  488.5 24.8 %all_gather.15 = bf16[256,384]{1,0:T(8,128)(2,1)S(1)} all-gather(bf16[32,384]{1,0:T(8,128)(2,1)S(1)} %fusion.41), channel_id=1, replica_groups=mesh['gx'=32,'gy'=8] {'gy'}, dimensions={0}, use_global_device_ids=true | all-gather | bytes 221184 | tf_op jit(solution)/shard_map/all_gather | solution.py:29
  516.4 9.7 %collective-permute-done.13 = bf16[512,384]{1,0:T(8,128)(2,1)S(1)} collective-permute-done((bf16[512,384]{1,0:T(8,128)(2,1)S(1)}, bf16[512,384]{1,0:T(8,128)(2,1)S(1)}, u32[]{:S(2)}, u32[]{:S(2)}) %collective-permute-start.13) | collective-permute-done | bytes 393248 | tf_op jit(solution)/shard_map/ppermute | solution.py:8
  529.5 17.2 %collective-permute-done.14 = bf16[1024,384]{1,0:T(8,128)(2,1)S(1)} collective-permute-done((bf16[1024,384]{1,0:T(8,128)(2,1)S(1)}, bf16[1024,384]{1,0:T(8,128)(2,1)S(1)}, u32[]{:S(2)}, u32[]{:S(2)}) %collective-permute-start.14) | collective-permute-done | bytes 786464 | tf_op jit(solution)/shard_map/ppermute | solution.py:8
  548.1 34.1 %collective-permute-done.15 = bf16[2048,384]{1,0:T(8,128)(2,1)S(1)} collective-permute-done((bf16[2048,384]{1,0:T(8,128)(2,1)S(1)}, bf16[2048,384]{1,0:T(8,128)(2,1)S(1)}, u32[]{:S(2)}, u32[]{:S(2)}) %collective-permute-start.15) | collective-permute-done | bytes 1572896 | tf_op jit(solution)/shard_map/ppermute | solution.py:8
  582.2 7.2 %maximum_select_fusion.11 = bf16[4096,384]{1,0:T(8,128)(2,1)S(1)} fusion(bf16[2048,384]{1,0:T(8,128)(2,1)S(1)} %maximum_select_fusion.14, bf16[2048,384]{1,0:T(8,128)(2,1)S(1)} %collective-permute-done.15, pred[]{:T(512)S(6)} %eq.15), kind=kLoop, calls=%fused_computation.41 | loop fusion | flops 14155776 | bytes 6291457 | tf_op jit(solution)/shard_map/jit(_where)/select_n | solution.py:34
  591.6 66.9 %collective-permute-done.16 = bf16[4096,384]{1,0:T(8,128)(2,1)S(1)} collective-permute-done((bf16[4096,384]{1,0:T(8,128)(2,1)S(1)}, bf16[4096,384]{1,0:T(8,128)(2,1)S(1)}, u32[]{:S(2)}, u32[]{:S(2)}) %collective-permute-start.16) | collective-permute-done | bytes 3145760 | tf_op jit(solution)/shard_map/ppermute | solution.py:8
  664.7 5.1 collective-permute-done.17
  (84 shorter events, 64.1 us)
Async XLA Ops:
  7.2 292.0 %copy-start = (bf16[128,8192]{1,0:T(8,128)(2,1)S(1)}, bf16[128,8192]{1,0:T(8,128)(2,1)}, u32[]{:S(2)}) copy-start(bf16[128,8192]{1,0:T(8,128)(2,1)} %param.20) | copy-start | bytes 6291460
  7.2 44.9 %all-gather.2.cloned.1.call-start = ((), (), s32[]{:S(2)}) async-start(), calls=%async_computation | async-start | bytes 1769472 | tf_op jit(solution)/shard_map/all_gather | solution.py:29
  52.1 3.8 collective-permute-start
  61.3 70.5 %collective-permute-start.1 = (bf16[4096,384]{1,0:T(8,128)(2,1)}, bf16[4096,384]{1,0:T(8,128)(2,1)}, u32[]{:S(2)}, u32[]{:S(2)}) collective-permute-start(bf16[4096,384]{1,0:T(8,128)(2,1)} %maximum_select_fusion.8), channel_id=1, source_target_pairs={{0,16},{8,24},{16,0},{24,8},{32,48},{40,56},{48,32},{56,40},{64,80... | collective-permute-start | bytes 9437192 | tf_op jit(solution)/shard_map/ppermute | solution.py:8
  140.8 11.9 %collective-permute-start.2 = (f32[256,384]{0,1:T(8,128)S(1)}, f32[256,384]{0,1:T(8,128)S(1)}, u32[]{:S(2)}, u32[]{:S(2)}) collective-permute-start(f32[256,384]{0,1:T(8,128)S(1)} %fusion.28), channel_id=1, source_target_pairs={{0,32},{8,40},{16,48},{24,56},{32,0},{40,8},{48,16},{56,24},{64,96... | collective-permute-start | bytes 1179656 | tf_op jit(solution)/shard_map/ppermute | solution.py:8
  180.5 2.3 collective-permute-start.3
  183.2 36.5 %collective-permute-start.4 = (bf16[2048,384]{1,0:T(8,128)(2,1)S(1)}, bf16[2048,384]{1,0:T(8,128)(2,1)S(1)}, u32[]{:S(2)}, u32[]{:S(2)}) collective-permute-start(bf16[2048,384]{1,0:T(8,128)(2,1)S(1)} %maximum_select_fusion.12), channel_id=1, source_target_pairs={{0,16},{8,24},{16,0},{24,8},{32,48},{40,56},{48,32},{56,40},{64,80... | collective-permute-start | bytes 4718600 | tf_op jit(solution)/shard_map/ppermute | solution.py:8
  228.0 71.1 %collective-permute-start.5 = (bf16[4096,384]{1,0:T(8,128)(2,1)}, bf16[4096,384]{1,0:T(8,128)(2,1)}, u32[]{:S(2)}, u32[]{:S(2)}) collective-permute-start(bf16[4096,384]{1,0:T(8,128)(2,1)} %maximum_select_fusion.9), channel_id=1, source_target_pairs={{0,32},{8,40},{16,48},{24,56},{32,0},{40,8},{48,16},{56,24},{64,96... | collective-permute-start | bytes 9437192 | tf_op jit(solution)/shard_map/ppermute | solution.py:8
  305.5 5.9 collective-permute-start.6
  338.4 1.7 collective-permute-start.7
  340.4 19.7 %collective-permute-start.8 = (bf16[1024,384]{1,0:T(8,128)(2,1)S(1)}, bf16[1024,384]{1,0:T(8,128)(2,1)S(1)}, u32[]{:S(2)}, u32[]{:S(2)}) collective-permute-start(bf16[1024,384]{1,0:T(8,128)(2,1)S(1)} %maximum_select_fusion.21), channel_id=1, source_target_pairs={{0,16},{8,24},{16,0},{24,8},{32,48},{40,56},{48,32},{56,40},{64,80... | collective-permute-start | bytes 2359304 | tf_op jit(solution)/shard_map/ppermute | solution.py:8
  360.5 114.2 %copy-start.6 = (bf16[64,8192]{1,0:T(8,128)(2,1)S(1)}, bf16[64,8192]{1,0:T(8,128)(2,1)}, u32[]{:S(2)}) copy-start(bf16[64,8192]{1,0:T(8,128)(2,1)} %param.21) | copy-start | bytes 3145732
  360.5 37.2 %collective-permute-start.9 = (bf16[2048,384]{1,0:T(8,128)(2,1)S(1)}, bf16[2048,384]{1,0:T(8,128)(2,1)S(1)}, u32[]{:S(2)}, u32[]{:S(2)}) collective-permute-start(bf16[2048,384]{1,0:T(8,128)(2,1)S(1)} %maximum_select_fusion.13), channel_id=1, source_target_pairs={{0,32},{8,40},{16,48},{24,56},{32,0},{40,8},{48,16},{56,24},{64,96... | collective-permute-start | bytes 4718600 | tf_op jit(solution)/shard_map/ppermute | solution.py:8
  406.0 68.7 %collective-permute-start.10 = (bf16[4096,384]{1,0:T(8,128)(2,1)}, bf16[4096,384]{1,0:T(8,128)(2,1)}, u32[]{:S(2)}, u32[]{:S(2)}) collective-permute-start(bf16[4096,384]{1,0:T(8,128)(2,1)} %maximum_select_fusion.10), channel_id=1, source_target_pairs={{0,64},{8,72},{16,80},{24,88},{32,96},{40,104},{48,112},{56,120},{... | collective-permute-start | bytes 9437192 | tf_op jit(solution)/shard_map/ppermute | solution.py:8
  480.9 6.2 collective-permute-start.11
  513.3 1.4 collective-permute-start.12
  514.9 11.2 %collective-permute-start.13 = (bf16[512,384]{1,0:T(8,128)(2,1)S(1)}, bf16[512,384]{1,0:T(8,128)(2,1)S(1)}, u32[]{:S(2)}, u32[]{:S(2)}) collective-permute-start(bf16[512,384]{1,0:T(8,128)(2,1)S(1)} %maximum_select_fusion.23), channel_id=1, source_target_pairs={{0,16},{8,24},{16,0},{24,8},{32,48},{40,56},{48,32},{56,40},{64,80... | collective-permute-start | bytes 1179656 | tf_op jit(solution)/shard_map/ppermute | solution.py:8
  526.4 20.3 %collective-permute-start.14 = (bf16[1024,384]{1,0:T(8,128)(2,1)S(1)}, bf16[1024,384]{1,0:T(8,128)(2,1)S(1)}, u32[]{:S(2)}, u32[]{:S(2)}) collective-permute-start(bf16[1024,384]{1,0:T(8,128)(2,1)S(1)} %maximum_select_fusion.22), channel_id=1, source_target_pairs={{0,32},{8,40},{16,48},{24,56},{32,0},{40,8},{48,16},{56,24},{64,96... | collective-permute-start | bytes 2359304 | tf_op jit(solution)/shard_map/ppermute | solution.py:8
  547.2 35.0 %collective-permute-start.15 = (bf16[2048,384]{1,0:T(8,128)(2,1)S(1)}, bf16[2048,384]{1,0:T(8,128)(2,1)S(1)}, u32[]{:S(2)}, u32[]{:S(2)}) collective-permute-start(bf16[2048,384]{1,0:T(8,128)(2,1)S(1)} %maximum_select_fusion.14), channel_id=1, source_target_pairs={{0,64},{8,72},{16,80},{24,88},{32,96},{40,104},{48,112},{56,120},{... | collective-permute-start | bytes 4718600 | tf_op jit(solution)/shard_map/ppermute | solution.py:8
  589.4 69.1 %collective-permute-start.16 = (bf16[4096,384]{1,0:T(8,128)(2,1)S(1)}, bf16[4096,384]{1,0:T(8,128)(2,1)S(1)}, u32[]{:S(2)}, u32[]{:S(2)}) collective-permute-start(bf16[4096,384]{1,0:T(8,128)(2,1)S(1)} %maximum_select_fusion.11), channel_id=1, source_target_pairs={{0,128},{8,136},{16,144},{24,152},{32,160},{40,168},{48,176},{56,1... | collective-permute-start | bytes 9437192 | tf_op jit(solution)/shard_map/ppermute | solution.py:8
  660.3 4.3 collective-permute-start.18
  662.3 7.5 %collective-permute-start.17 = (f32[2,1,16,384]{3,2,1,0:T(8,128)S(1)}, f32[2,1,16,384]{3,2,1,0:T(8,128)S(1)}, u32[]{:S(2)}, u32[]{:S(2)}) collective-permute-start(f32[2,1,16,384]{3,2,1,0:T(8,128)S(1)} %get-tuple-element.27), channel_id=1, source_target_pairs={{0,8},{8,16},{16,24},{24,32},{32,40},{40,48},{48,56},{56,64},{64,7... | collective-permute-start | bytes 147464 | tf_op jit(solution)/shard_map/ppermute | solution.py:19
  669.8 5.9 collective-permute-start.20
  673.1 5.6 collective-permute-start.19
  (6 other events, 300.0 us)
Sparse Core Ops, SparseCore 0:
  9.8 42.2 all-gather.1
where the time goes:
time: 687 us; the launch traced here: 686 us
  waiting for transfers between devices  498 us (72%)
  blocking collectives  75.7 us (11%)
  starting transfers between devices  35.3 us (5%)
  other arithmetic  32.4 us (5%)
  matrix products  23.4 us (3%)
  between operations  14.4 us (2%)
  local copies, waits for them, and re-layouts  6.91 us (1%)
    ppermute x17, waiting for transfers between devices, swapped(): lax.ppermute(x, axis, [(i, i ^ 1 << distance) for i in range(lax.axis_siz...  445 us
    all_gather x3, blocking collectives, group_rows(): values = lax.all_gather(values, 'gy', axis=0, tiled=True)  75.7 us
    all_gather x1, waiting for transfers between devices, group_rows(): values = lax.all_gather(values, 'gy', axis=0, tiled=True)  44.2 us
    select_n x10, other arithmetic, group_rows(): jnp.where(upper, jnp.concatenate([other, values], 0), jnp.concatenate([va...  31.2 us
    ppermute x17, starting transfers between devices, swapped(): lax.ppermute(x, axis, [(i, i ^ 1 << distance) for i in range(lax.axis_siz...  25.1 us
    dot_general x3, matrix products, local(): product = jnp.dot(fronts[level], whole, preferred_element_type=jnp.float32)  21.6 us
  transfers between devices with their start and end apart: 22, of which 20 were waited for; matrix products, arithmetic and copies ran while one was open for 0% of the time, Pallas kernels for 0%

commit v1 on v0

--- a/solution.py
+++ b/solution.py
@@ -26,7 +26,9 @@
 
 
 def group_rows(values, bits):
-    values = lax.all_gather(values, "gy", axis=0, tiled=True)
+    values = jnp.concatenate(
+        lax.all_to_all(jnp.stack([values] * lax.axis_size("gy")), "gy", 0, 0), axis=0
+    )
     column = lax.axis_index("gx")
     for bit in range(bits):
         other = swapped(values, "gx", bit)

time: 687 us -> 652 us (0.949)
  waiting for transfers between devices: 498 us -> 452 us
  blocking collectives: 75.7 us -> 98.3 us
  between operations: 14.4 us -> 1 us
    all_to_all x0 -> x4, blocking collectives: none -> 98.3 us  [group_rows(): lax.all_to_all(jnp.stack([values] * lax.axis_size('gy')), 'gy', 0, 0)]
    all_gather x3 -> x0, blocking collectives: 75.7 us -> none  [group_rows(): values = lax.all_gather(values, 'gy', axis=0, tiled=True)]
    all_gather x1 -> x0, waiting for transfers between devices: 44.2 us -> none  [group_rows(): values = lax.all_gather(values, 'gy', axis=0, tiled=True)]
  transfers between devices with their start and end apart: 22 -> 21, of which waited for: 20 -> 19; matrix products, arithmetic and copies ran while one was open for 0% -> 0% of each run, Pallas kernels for 0% -> 0%
where the time goes in v1:
time: 652 us
  waiting for transfers between devices  452 us (69%)
  blocking collectives  98.3 us (15%)
  starting transfers between devices  36.3 us (6%)
  other arithmetic  32.3 us (5%)
  matrix products  23.3 us (4%)
  local copies, waits for them, and re-layouts  8.24 us (1%)
    ppermute x17, waiting for transfers between devices, swapped(): lax.ppermute(x, axis, [(i, i ^ 1 << distance) for i in range(lax.axis_siz...  444 us
    all_to_all x4, blocking collectives, group_rows(): lax.all_to_all(jnp.stack([values] * lax.axis_size('gy')), 'gy', 0, 0)  98.3 us
    select_n x10, other arithmetic, group_rows(): jnp.where(upper, jnp.concatenate([other, values], 0), jnp.concatenate([va...  31.1 us
    ppermute x17, starting transfers between devices, swapped(): lax.ppermute(x, axis, [(i, i ^ 1 << distance) for i in range(lax.axis_siz...  26.2 us
    dot_general x3, matrix products, local(): product = jnp.dot(fronts[level], whole, preferred_element_type=jnp.float32)  21.5 us
  transfers between devices with their start and end apart: 21, of which 19 were waited for; matrix products, arithmetic and copies ran while one was open for 0% of the time, Pallas kernels for 0%

profile of v1, /device:TPU:34, one launch (start us, length us, event | category | flops | bytes accessed | tf_op | source)
XLA Modules:
  0.0 651.8 jit_solution(12825064988890354405)
XLA Ops:
  1.9 47.0 %all_to_all.20 = bf16[8,256,384]{2,1,0:T(8,128)(2,1)} all-to-all(bf16[8,256,384]{2,1,0:T(8,128)(2,1)S(1)} %stack.12), channel_id=1, replica_groups=mesh['gx'=32,'gy'=8] {'gy'}, dimensions={0} | all-to-all | bytes 3145728 | tf_op jit(solution)/shard_map/all_to_all | solution.py:30
  52.6 5.4 maximum_select_fusion.8
  59.6 68.9 %collective-permute-done.1 = bf16[4096,384]{1,0:T(8,128)(2,1)} collective-permute-done((bf16[4096,384]{1,0:T(8,128)(2,1)}, bf16[4096,384]{1,0:T(8,128)(2,1)}, u32[]{:S(2)}, u32[]{:S(2)}) %collective-permute-start.1) | collective-permute-done | bytes 3145760 | tf_op jit(solution)/shard_map/ppermute | solution.py:8
  128.5 9.0 %fusion.28 = f32[256,384]{0,1:T(8,128)S(1)} fusion(bf16[256,8192]{1,0:T(8,128)(2,1)} %param.19, bf16[4096,384]{1,0:T(8,128)(2,1)} %maximum_select_fusion.8, bf16[4096,384]{1,0:T(8,128)(2,1)} %collective-permute-done.1, pred[]{:T(512)S(6)} %eq.17), kind=kOutput, calls=%fused_computation.45 | convolution fusion | flops 1638924288 | bytes 10878977 | tf_op jit(solution)/shard_map/dot_general | solution.py:66
  141.5 7.9 %collective-permute-done.2 = f32[256,384]{0,1:T(8,128)S(1)} collective-permute-done((f32[256,384]{0,1:T(8,128)S(1)}, f32[256,384]{0,1:T(8,128)S(1)}, u32[]{:S(2)}, u32[]{:S(2)}) %collective-permute-start.2) | collective-permute-done | bytes 393248 | tf_op jit(solution)/shard_map/ppermute | solution.py:8
  151.6 24.4 %all_to_all.21 = bf16[8,128,384]{2,1,0:T(8,128)(2,1)S(1)} all-to-all(bf16[8,128,384]{2,1,0:T(8,128)(2,1)S(1)} %stack.13), channel_id=1, replica_groups=mesh['gx'=32,'gy'=8] {'gy'}, dimensions={0} | all-to-all | bytes 1572864 | tf_op jit(solution)/shard_map/all_to_all | solution.py:30
  180.3 34.9 %collective-permute-done.4 = bf16[2048,384]{1,0:T(8,128)(2,1)S(1)} collective-permute-done((bf16[2048,384]{1,0:T(8,128)(2,1)S(1)}, bf16[2048,384]{1,0:T(8,128)(2,1)S(1)}, u32[]{:S(2)}, u32[]{:S(2)}) %collective-permute-start.4) | collective-permute-done | bytes 1572896 | tf_op jit(solution)/shard_map/ppermute | solution.py:8
  215.2 8.2 %maximum_select_fusion.9 = bf16[4096,384]{1,0:T(8,128)(2,1)} fusion(bf16[2048,384]{1,0:T(8,128)(2,1)S(1)} %maximum_select_fusion.12, bf16[2048,384]{1,0:T(8,128)(2,1)S(1)} %collective-permute-done.4, pred[]{:T(512)S(6)} %eq.17), kind=kLoop, calls=%fused_computation.39 | loop fusion | flops 14155776 | bytes 6291457 | tf_op jit(solution)/shard_map/jit(_where)/select_n | solution.py:36
  227.3 67.2 %collective-permute-done.5 = bf16[4096,384]{1,0:T(8,128)(2,1)} collective-permute-done((bf16[4096,384]{1,0:T(8,128)(2,1)}, bf16[4096,384]{1,0:T(8,128)(2,1)}, u32[]{:S(2)}, u32[]{:S(2)}) %collective-permute-start.5) | collective-permute-done | bytes 3145760 | tf_op jit(solution)/shard_map/ppermute | solution.py:8
  294.5 6.3 fusion.29
  301.7 5.1 collective-permute-done.6
  308.6 14.6 %all_to_all.22 = bf16[8,64,384]{2,1,0:T(8,128)(2,1)S(1)} all-to-all(bf16[8,64,384]{2,1,0:T(8,128)(2,1)S(1)} %stack.14), channel_id=1, replica_groups=mesh['gx'=32,'gy'=8] {'gy'}, dimensions={0} | all-to-all | bytes 786432 | tf_op jit(solution)/shard_map/all_to_all | solution.py:30
  326.8 18.0 %collective-permute-done.8 = bf16[1024,384]{1,0:T(8,128)(2,1)S(1)} collective-permute-done((bf16[1024,384]{1,0:T(8,128)(2,1)S(1)}, bf16[1024,384]{1,0:T(8,128)(2,1)S(1)}, u32[]{:S(2)}, u32[]{:S(2)}) %collective-permute-start.8) | collective-permute-done | bytes 786464 | tf_op jit(solution)/shard_map/ppermute | solution.py:8
  348.6 33.9 %collective-permute-done.9 = bf16[2048,384]{1,0:T(8,128)(2,1)S(1)} collective-permute-done((bf16[2048,384]{1,0:T(8,128)(2,1)S(1)}, bf16[2048,384]{1,0:T(8,128)(2,1)S(1)}, u32[]{:S(2)}, u32[]{:S(2)}) %collective-permute-start.9) | collective-permute-done | bytes 1572896 | tf_op jit(solution)/shard_map/ppermute | solution.py:8
  382.5 8.2 %maximum_select_fusion.10 = bf16[4096,384]{1,0:T(8,128)(2,1)} fusion(bf16[2048,384]{1,0:T(8,128)(2,1)S(1)} %maximum_select_fusion.13, bf16[2048,384]{1,0:T(8,128)(2,1)S(1)} %collective-permute-done.9, pred[]{:T(512)S(6)} %eq.16), kind=kLoop, calls=%fused_computation.40 | loop fusion | flops 14155776 | bytes 6291457 | tf_op jit(solution)/shard_map/jit(_where)/select_n | solution.py:36
  392.0 67.4 %collective-permute-done.10 = bf16[4096,384]{1,0:T(8,128)(2,1)} collective-permute-done((bf16[4096,384]{1,0:T(8,128)(2,1)}, bf16[4096,384]{1,0:T(8,128)(2,1)}, u32[]{:S(2)}, u32[]{:S(2)}) %collective-permute-start.10) | collective-permute-done | bytes 3145760 | tf_op jit(solution)/shard_map/ppermute | solution.py:8
  459.5 6.2 fusion.30
  473.2 12.4 %all_to_all.23 = bf16[8,32,384]{2,1,0:T(8,128)(2,1)S(1)} all-to-all(bf16[8,32,384]{2,1,0:T(8,128)(2,1)S(1)} %stack.15), channel_id=1, replica_groups=mesh['gx'=32,'gy'=8] {'gy'}, dimensions={0} | all-to-all | bytes 393216 | tf_op jit(solution)/shard_map/all_to_all | solution.py:30
  488.8 9.6 %collective-permute-done.13 = bf16[512,384]{1,0:T(8,128)(2,1)S(1)} collective-permute-done((bf16[512,384]{1,0:T(8,128)(2,1)S(1)}, bf16[512,384]{1,0:T(8,128)(2,1)S(1)}, u32[]{:S(2)}, u32[]{:S(2)}) %collective-permute-start.13) | collective-permute-done | bytes 393248 | tf_op jit(solution)/shard_map/ppermute | solution.py:8
  502.0 17.1 %collective-permute-done.14 = bf16[1024,384]{1,0:T(8,128)(2,1)S(1)} collective-permute-done((bf16[1024,384]{1,0:T(8,128)(2,1)S(1)}, bf16[1024,384]{1,0:T(8,128)(2,1)S(1)}, u32[]{:S(2)}, u32[]{:S(2)}) %collective-permute-start.14) | collective-permute-done | bytes 786464 | tf_op jit(solution)/shard_map/ppermute | solution.py:8
  520.3 34.2 %collective-permute-done.15 = bf16[2048,384]{1,0:T(8,128)(2,1)S(1)} collective-permute-done((bf16[2048,384]{1,0:T(8,128)(2,1)S(1)}, bf16[2048,384]{1,0:T(8,128)(2,1)S(1)}, u32[]{:S(2)}, u32[]{:S(2)}) %collective-permute-start.15) | collective-permute-done | bytes 1572896 | tf_op jit(solution)/shard_map/ppermute | solution.py:8
  554.5 7.2 %maximum_select_fusion.11 = bf16[4096,384]{1,0:T(8,128)(2,1)S(1)} fusion(bf16[2048,384]{1,0:T(8,128)(2,1)S(1)} %maximum_select_fusion.14, bf16[2048,384]{1,0:T(8,128)(2,1)S(1)} %collective-permute-done.15, pred[]{:T(512)S(6)} %eq.15), kind=kLoop, calls=%fused_computation.41 | loop fusion | flops 14155776 | bytes 6291457 | tf_op jit(solution)/shard_map/jit(_where)/select_n | solution.py:36
  563.9 66.9 %collective-permute-done.16 = bf16[4096,384]{1,0:T(8,128)(2,1)S(1)} collective-permute-done((bf16[4096,384]{1,0:T(8,128)(2,1)S(1)}, bf16[4096,384]{1,0:T(8,128)(2,1)S(1)}, u32[]{:S(2)}, u32[]{:S(2)}) %collective-permute-start.16) | collective-permute-done | bytes 3145760 | tf_op jit(solution)/shard_map/ppermute | solution.py:8
  637.0 5.1 collective-permute-done.17
  (86 shorter events, 65.9 us)
Async XLA Ops:
  0.6 293.9 %copy-start = (bf16[128,8192]{1,0:T(8,128)(2,1)S(1)}, bf16[128,8192]{1,0:T(8,128)(2,1)}, u32[]{:S(2)}) copy-start(bf16[128,8192]{1,0:T(8,128)(2,1)} %param.20) | copy-start | bytes 6291460
  48.8 3.8 collective-permute-start
  58.0 70.5 %collective-permute-start.1 = (bf16[4096,384]{1,0:T(8,128)(2,1)}, bf16[4096,384]{1,0:T(8,128)(2,1)}, u32[]{:S(2)}, u32[]{:S(2)}) collective-permute-start(bf16[4096,384]{1,0:T(8,128)(2,1)} %maximum_select_fusion.8), channel_id=1, source_target_pairs={{0,16},{8,24},{16,0},{24,8},{32,48},{40,56},{48,32},{56,40},{64,80... | collective-permute-start | bytes 9437192 | tf_op jit(solution)/shard_map/ppermute | solution.py:8
  137.5 11.9 %collective-permute-start.2 = (f32[256,384]{0,1:T(8,128)S(1)}, f32[256,384]{0,1:T(8,128)S(1)}, u32[]{:S(2)}, u32[]{:S(2)}) collective-permute-start(f32[256,384]{0,1:T(8,128)S(1)} %fusion.28), channel_id=1, source_target_pairs={{0,32},{8,40},{16,48},{24,56},{32,0},{40,8},{48,16},{56,24},{64,96... | collective-permute-start | bytes 1179656 | tf_op jit(solution)/shard_map/ppermute | solution.py:8
  175.9 2.3 collective-permute-start.3
  178.6 36.5 %collective-permute-start.4 = (bf16[2048,384]{1,0:T(8,128)(2,1)S(1)}, bf16[2048,384]{1,0:T(8,128)(2,1)S(1)}, u32[]{:S(2)}, u32[]{:S(2)}) collective-permute-start(bf16[2048,384]{1,0:T(8,128)(2,1)S(1)} %maximum_select_fusion.12), channel_id=1, source_target_pairs={{0,16},{8,24},{16,0},{24,8},{32,48},{40,56},{48,32},{56,40},{64,80... | collective-permute-start | bytes 4718600 | tf_op jit(solution)/shard_map/ppermute | solution.py:8
  223.4 71.1 %collective-permute-start.5 = (bf16[4096,384]{1,0:T(8,128)(2,1)}, bf16[4096,384]{1,0:T(8,128)(2,1)}, u32[]{:S(2)}, u32[]{:S(2)}) collective-permute-start(bf16[4096,384]{1,0:T(8,128)(2,1)} %maximum_select_fusion.9), channel_id=1, source_target_pairs={{0,32},{8,40},{16,48},{24,56},{32,0},{40,8},{48,16},{56,24},{64,96... | collective-permute-start | bytes 9437192 | tf_op jit(solution)/shard_map/ppermute | solution.py:8
  300.9 5.9 collective-permute-start.6
  323.1 1.7 collective-permute-start.7
  325.2 19.7 %collective-permute-start.8 = (bf16[1024,384]{1,0:T(8,128)(2,1)S(1)}, bf16[1024,384]{1,0:T(8,128)(2,1)S(1)}, u32[]{:S(2)}, u32[]{:S(2)}) collective-permute-start(bf16[1024,384]{1,0:T(8,128)(2,1)S(1)} %maximum_select_fusion.21), channel_id=1, source_target_pairs={{0,16},{8,24},{16,0},{24,8},{32,48},{40,56},{48,32},{56,40},{64,80... | collective-permute-start | bytes 2359304 | tf_op jit(solution)/shard_map/ppermute | solution.py:8
  345.3 114.2 %copy-start.6 = (bf16[64,8192]{1,0:T(8,128)(2,1)S(1)}, bf16[64,8192]{1,0:T(8,128)(2,1)}, u32[]{:S(2)}) copy-start(bf16[64,8192]{1,0:T(8,128)(2,1)} %param.21) | copy-start | bytes 3145732
  345.3 37.2 %collective-permute-start.9 = (bf16[2048,384]{1,0:T(8,128)(2,1)S(1)}, bf16[2048,384]{1,0:T(8,128)(2,1)S(1)}, u32[]{:S(2)}, u32[]{:S(2)}) collective-permute-start(bf16[2048,384]{1,0:T(8,128)(2,1)S(1)} %maximum_select_fusion.13), channel_id=1, source_target_pairs={{0,32},{8,40},{16,48},{24,56},{32,0},{40,8},{48,16},{56,24},{64,96... | collective-permute-start | bytes 4718600 | tf_op jit(solution)/shard_map/ppermute | solution.py:8
  390.7 68.7 %collective-permute-start.10 = (bf16[4096,384]{1,0:T(8,128)(2,1)}, bf16[4096,384]{1,0:T(8,128)(2,1)}, u32[]{:S(2)}, u32[]{:S(2)}) collective-permute-start(bf16[4096,384]{1,0:T(8,128)(2,1)} %maximum_select_fusion.10), channel_id=1, source_target_pairs={{0,64},{8,72},{16,80},{24,88},{32,96},{40,104},{48,112},{56,120},{... | collective-permute-start | bytes 9437192 | tf_op jit(solution)/shard_map/ppermute | solution.py:8
  465.6 6.2 collective-permute-start.11
  485.6 1.4 collective-permute-start.12
  487.2 11.2 %collective-permute-start.13 = (bf16[512,384]{1,0:T(8,128)(2,1)S(1)}, bf16[512,384]{1,0:T(8,128)(2,1)S(1)}, u32[]{:S(2)}, u32[]{:S(2)}) collective-permute-start(bf16[512,384]{1,0:T(8,128)(2,1)S(1)} %maximum_select_fusion.23), channel_id=1, source_target_pairs={{0,16},{8,24},{16,0},{24,8},{32,48},{40,56},{48,32},{56,40},{64,80... | collective-permute-start | bytes 1179656 | tf_op jit(solution)/shard_map/ppermute | solution.py:8
  498.7 20.3 %collective-permute-start.14 = (bf16[1024,384]{1,0:T(8,128)(2,1)S(1)}, bf16[1024,384]{1,0:T(8,128)(2,1)S(1)}, u32[]{:S(2)}, u32[]{:S(2)}) collective-permute-start(bf16[1024,384]{1,0:T(8,128)(2,1)S(1)} %maximum_select_fusion.22), channel_id=1, source_target_pairs={{0,32},{8,40},{16,48},{24,56},{32,0},{40,8},{48,16},{56,24},{64,96... | collective-permute-start | bytes 2359304 | tf_op jit(solution)/shard_map/ppermute | solution.py:8
  519.5 111.3 %copy-start.7 = (bf16[32,8192]{1,0:T(8,128)(2,1)S(1)}, bf16[32,8192]{1,0:T(8,128)(2,1)}, u32[]{:S(2)}) copy-start(bf16[32,8192]{1,0:T(8,128)(2,1)} %param.22) | copy-start | bytes 1572868
  519.5 35.0 %collective-permute-start.15 = (bf16[2048,384]{1,0:T(8,128)(2,1)S(1)}, bf16[2048,384]{1,0:T(8,128)(2,1)S(1)}, u32[]{:S(2)}, u32[]{:S(2)}) collective-permute-start(bf16[2048,384]{1,0:T(8,128)(2,1)S(1)} %maximum_select_fusion.14), channel_id=1, source_target_pairs={{0,64},{8,72},{16,80},{24,88},{32,96},{40,104},{48,112},{56,120},{... | collective-permute-start | bytes 4718600 | tf_op jit(solution)/shard_map/ppermute | solution.py:8
  561.7 69.1 %collective-permute-start.16 = (bf16[4096,384]{1,0:T(8,128)(2,1)S(1)}, bf16[4096,384]{1,0:T(8,128)(2,1)S(1)}, u32[]{:S(2)}, u32[]{:S(2)}) collective-permute-start(bf16[4096,384]{1,0:T(8,128)(2,1)S(1)} %maximum_select_fusion.11), channel_id=1, source_target_pairs={{0,128},{8,136},{16,144},{24,152},{32,160},{40,168},{48,176},{56,1... | collective-permute-start | bytes 9437192 | tf_op jit(solution)/shard_map/ppermute | solution.py:8
  632.6 4.3 collective-permute-start.18
  634.6 7.5 %collective-permute-start.17 = (f32[2,1,16,384]{3,2,1,0:T(8,128)S(1)}, f32[2,1,16,384]{3,2,1,0:T(8,128)S(1)}, u32[]{:S(2)}, u32[]{:S(2)}) collective-permute-start(f32[2,1,16,384]{3,2,1,0:T(8,128)S(1)} %get-tuple-element.27), channel_id=1, source_target_pairs={{0,8},{8,16},{16,24},{24,32},{32,40},{40,48},{48,56},{56,64},{64,7... | collective-permute-start | bytes 147464 | tf_op jit(solution)/shard_map/ppermute | solution.py:19
  642.1 5.9 collective-permute-start.20
  645.5 5.6 collective-permute-start.19
  (5 other events, 188.6 us)
